TPU v7x, 256 devices: a whole 4x4x8 slice. The times are simulated.
256 devices in a mesh: req: 8 (over z), exp: 8 (over y, core), hid: 4 (over x).
Axes of the slice: x: 4, y: 4, z: 8, core: 2. Of those that a mesh axis runs over, the one named last changes fastest.
Arguments:
- layer_input_rows: bfloat16 [16384, 1536], P(('req', 'exp')), may hold values from -6 to 6
- attention_norm_gain: float32 [1536], replicated
- query_weight: bfloat16 [1536, 1536], P(None, 'hid'), may hold values from -1 to 1
- key_weight: bfloat16 [1536, 512], P(None, 'hid'), may hold values from -1 to 1
- value_weight: bfloat16 [1536, 512], P(None, 'hid'), may hold values from -0.15625 to 0.15625
- attention_output_weight: bfloat16 [1536, 1536], P('hid'), may hold values from -0.15625 to 0.15625
- query_down_factor: bfloat16 [64, 1536, 16], P(('req', 'exp')), may hold values from -0.15625 to 0.15625
- query_up_factor: bfloat16 [64, 16, 1536], P(('req', 'exp')), may hold values from -1.5 to 1.5
- value_down_factor: bfloat16 [64, 1536, 16], P(('req', 'exp')), may hold values from -0.15625 to 0.15625
- value_up_factor: bfloat16 [64, 16, 512], P(('req', 'exp')), may hold values from -1.5 to 1.5
- lengths: int32 [8, 4], P('req'), may hold values from 1 to 1024, 2048 in all within a row
- request_adapter: int32 [8, 4], replicated, may hold values from 0 to 63
- adapter_home_row: int32 [64], replicated, may hold values from 0 to 63, each once
- expert_norm_gain: float32 [1536], replicated, may hold values from 0.4 to 1.6
- routes: int32 [16384, 8], P(('req', 'exp', 'hid')), may hold values from 0 to 39, all different within a row; in each aligned block of 64 rows (0 to 63, 64 to 127, ...) at most 16 rows name the same one
- router_expert_weight: float32 [16384, 8], P(('req', 'exp', 'hid')), may hold values from 0.1 to 0.5
- expert_gate_weight: bfloat16 [40, 1536, 512], P('exp', None, 'hid'), may hold values from -0.15625 to 0.15625
- expert_up_weight: bfloat16 [40, 1536, 512], P('exp', None, 'hid'), may hold values from -0.15625 to 0.15625
- expert_down_weight: bfloat16 [40, 512, 1536], P('exp', 'hid'), may hold values from -0.25 to 0.25
Outputs:
- attn_out: bfloat16 [16384, 1536], P(('req', 'exp', 'hid'))
- expert_out: bfloat16 [16384, 1536], P(('req', 'exp', 'hid'))
Inputs may be any that keep to these rules, and one draw needn't show every extreme that they name: `lengths`: each row sums to 2048; its largest entry is exactly 1024. `adapter_home_row`: each adapter row appears once. `routes`: A row names 8 different experts. In the rows of one device (64 consecutive rows, aligned) no expert is named more than 16 times, a bound that some block reaches in some of them.
All inputs are finite; a program needn't handle non-finite values.
Results may differ from a plain program's by a relative error of at most 0.029.
The roundings to bfloat16 on the way count: a program that leaves them out, or rounds other values in their place, can miss the bound.
Values may be sent and summed in bfloat16 or wider, within the bound.
No kernel may reach another device: no remote copies, remote signals or barrier semaphores. Data moves between devices by JAX's collectives and lax.ppermute only.
A program may use at most 128 MiB of HBM per device.

v0:
```python
import jax
import jax.numpy as jnp
from jax import lax
from jax.sharding import PartitionSpec as P

HEAD_WIDTH = 64
scale_attn = 0.015625
residual_mult = 0.22
norm_eps = 1e-06
rope_base = 10000.0
neg_large = -1e30


def rms_norm(values, norm_gain):
    widened = values.astype(jnp.float32)
    mean_sq = jnp.mean(widened * widened, axis=-1, keepdims=True)
    return (widened * lax.rsqrt(mean_sq + norm_eps) * norm_gain).astype(jnp.bfloat16)


def rotary(heads_in, position):
    half_size = heads_in.shape[-1] // 2
    frequency = rope_base ** (-2.0 * jnp.arange(half_size, dtype=jnp.float32) / heads_in.shape[-1])
    angles = position.astype(jnp.float32)[:, None] * frequency[None, :]
    cosine = jnp.cos(angles)[:, None, :]
    sine_part = jnp.sin(angles)[:, None, :]
    first_half = heads_in[..., :half_size]
    second_half = heads_in[..., half_size:]
    return jnp.concatenate(
        [
            first_half * cosine - second_half * sine_part,
            second_half * cosine + first_half * sine_part,
        ],
        axis=-1,
    )


def request_of(row_ids, group_len):
    request_end = jnp.cumsum(group_len)
    return jnp.sum((row_ids[:, None] >= request_end[None, :]).astype(jnp.int32), axis=1)


def locate(row_ids, group_len):
    request_end = jnp.cumsum(group_len)
    request_start = request_end - group_len
    request = request_of(row_ids, group_len)
    member = request[:, None] == jnp.arange(group_len.shape[0], dtype=jnp.int32)[None, :]
    position = row_ids - jnp.sum(jnp.where(member, request_start[None, :], 0), axis=1)
    return (request, member, position)


def expert_rows(rows_in, expert_gate_weight, expert_up_weight, expert_down_weight):
    gate_act = jnp.einsum(
        "red,edf->ref", rows_in, expert_gate_weight, preferred_element_type=jnp.float32
    )
    upper = jnp.einsum(
        "red,edf->ref", rows_in, expert_up_weight, preferred_element_type=jnp.float32
    )
    hidden = (jax.nn.silu(gate_act) * upper).astype(jnp.bfloat16)
    return jnp.einsum(
        "ref,efd->red", hidden, expert_down_weight, preferred_element_type=jnp.float32
    )


def per_device(
    layer_input_rows,
    attention_norm_gain,
    query_weight,
    key_weight,
    value_weight,
    attention_output_weight,
    query_down_factor,
    query_up_factor,
    value_down_factor,
    value_up_factor,
    lengths,
    request_adapter,
    adapter_home_row,
    expert_norm_gain,
    routes,
    router_expert_weight,
    expert_gate_weight,
    expert_up_weight,
    expert_down_weight,
):
    exp_count = lax.axis_size("exp")
    hid_count = lax.axis_size("hid")
    exp_index = lax.axis_index("exp")
    hid_index = lax.axis_index("hid")
    req_index = lax.axis_index("req")
    query_rows = layer_input_rows.shape[0]
    width = layer_input_rows.shape[1]
    kv_local = key_weight.shape[1] // HEAD_WIDTH
    q_local = query_weight.shape[1] // HEAD_WIDTH
    group_share = q_local // kv_local
    adapter_rank_size = query_down_factor.shape[2]
    requests = lengths.shape[1]
    group_len = lengths[0]
    row_ids = exp_index * query_rows + jnp.arange(query_rows, dtype=jnp.int32)
    request, member, position = locate(row_ids, group_len)
    wanted = lax.dynamic_index_in_dim(request_adapter, req_index, 0, keepdims=False)
    slot_ids = jnp.arange(adapter_home_row.shape[0], dtype=jnp.int32)
    home_of = jnp.sum(
        jnp.where(wanted[:, None] == slot_ids[None, :], adapter_home_row[None, :], 0), axis=1
    )
    pieces = (
        lax.all_gather(query_down_factor, ("req", "exp"), axis=0, tiled=True),
        lax.all_gather(query_up_factor, ("req", "exp"), axis=0, tiled=True),
        lax.all_gather(value_down_factor, ("req", "exp"), axis=0, tiled=True),
        lax.all_gather(value_up_factor, ("req", "exp"), axis=0, tiled=True),
    )
    adapter_bank_rows = jnp.arange(pieces[0].shape[0], dtype=jnp.int32)
    selector = (home_of[:, None] == adapter_bank_rows[None, :]).astype(jnp.bfloat16)
    picked_now = tuple(
        (
            jnp.einsum("jn,nab->jab", selector, piece_in, preferred_element_type=jnp.float32)
            for piece_in in pieces
        )
    )
    chosen = tuple((fresh for fresh in picked_now))
    qa_sel, qb_sel, va_sel, vb_sel = [member_in.astype(jnp.bfloat16) for member_in in chosen]
    normed_rows = rms_norm(layer_input_rows, attention_norm_gain)

    def low_rank_term(a_sel, b_sel, width_cols, offset):
        inner_terms = jnp.einsum(
            "td,jdr->tjr", normed_rows, a_sel, preferred_element_type=jnp.float32
        )
        inner_terms = (
            jnp.where(member[:, :, None], inner_terms, 0.0)
            .reshape(query_rows, requests * adapter_rank_size)
            .astype(jnp.bfloat16)
        )
        right_factor = lax.dynamic_slice_in_dim(b_sel, offset, width_cols, 2).reshape(
            requests * adapter_rank_size, width_cols
        )
        return jnp.dot(inner_terms, right_factor, preferred_element_type=jnp.float32)

    query_cols = q_local * HEAD_WIDTH
    kv_cols = kv_local * HEAD_WIDTH
    query_matrix = jnp.dot(
        normed_rows, query_weight, preferred_element_type=jnp.float32
    ) + low_rank_term(qa_sel, qb_sel, query_cols, hid_index * query_cols)
    query_matrix = rotary(query_matrix.reshape(query_rows, q_local, HEAD_WIDTH), position).astype(
        jnp.bfloat16
    )
    query_matrix = query_matrix.reshape(query_rows, kv_local, group_share, HEAD_WIDTH)
    keys_own = jnp.dot(normed_rows, key_weight, preferred_element_type=jnp.float32)
    keys_own = (
        rotary(keys_own.reshape(query_rows, kv_local, HEAD_WIDTH), position)
        .astype(jnp.bfloat16)
        .reshape(query_rows, kv_cols)
    )
    values_own = jnp.dot(
        normed_rows, value_weight, preferred_element_type=jnp.float32
    ) + low_rank_term(va_sel, vb_sel, kv_cols, hid_index * kv_cols)
    values_own = values_own.astype(jnp.bfloat16)
    running_max = jnp.full((kv_local, group_share, query_rows), neg_large, jnp.float32)
    key_piece = lax.all_gather(keys_own, "exp", axis=0, tiled=True)
    value_piece = lax.all_gather(values_own, "exp", axis=0, tiled=True)
    piece_len = key_piece.shape[0]
    key_ids = jnp.arange(piece_len, dtype=jnp.int32)
    key_request = request_of(key_ids, group_len)
    allowed = (request[:, None] == key_request[None, :]) & (key_ids[None, :] <= row_ids[:, None])
    key_heads = key_piece.reshape(piece_len, kv_local, HEAD_WIDTH)
    value_heads = value_piece.reshape(piece_len, kv_local, HEAD_WIDTH)
    scores = (
        jnp.einsum("qkgh,nkh->kgqn", query_matrix, key_heads, preferred_element_type=jnp.float32)
        * scale_attn
    )
    scores = jnp.where(allowed[None, None], scores, neg_large)
    new_max = jnp.maximum(running_max, jnp.max(scores, axis=-1))
    weights = jnp.where(allowed[None, None], jnp.exp(scores - new_max[..., None]), 0.0)
    running_sum = jnp.sum(weights, axis=-1)
    running_out = jnp.einsum(
        "kgqn,nkh->kgqh",
        weights.astype(jnp.bfloat16),
        value_heads,
        preferred_element_type=jnp.float32,
    )
    running_max, running_sum, running_out = (new_max, running_sum, running_out)
    attended = (running_out / running_sum[..., None]).astype(jnp.bfloat16)
    attended = jnp.transpose(attended, (2, 0, 1, 3)).reshape(query_rows, query_cols)
    tok_rows = query_rows // hid_count
    attn_out = lax.psum_scatter(
        jnp.dot(attended, attention_output_weight, preferred_element_type=jnp.float32).astype(
            jnp.bfloat16
        ),
        "hid",
        scatter_dimension=0,
        tiled=True,
    )
    own_rows = lax.dynamic_slice_in_dim(layer_input_rows, hid_index * tok_rows, tok_rows, 0)
    mixed_rows = own_rows.astype(jnp.float32) + residual_mult * attn_out.astype(jnp.float32)
    normed_moe = rms_norm(mixed_rows, expert_norm_gain)
    local_exp = expert_gate_weight.shape[0]
    expert_count = local_exp * exp_count
    top_count = routes.shape[1]
    capacity = max(2, tok_rows // 4)
    flat_route = routes.reshape(tok_rows * top_count)
    route_hits = (flat_route[:, None] == jnp.arange(expert_count, dtype=jnp.int32)[None, :]).astype(
        jnp.int32
    )
    earlier = jnp.cumsum(route_hits, axis=0) - route_hits
    slot_pos = jnp.sum(earlier * route_hits, axis=1)
    slots = slot_pos * expert_count + flat_route
    slot_table = jnp.arange(capacity * expert_count, dtype=jnp.int32)
    placed = jnp.any(
        slot_table[:, None, None] == slots.reshape(tok_rows, top_count)[None], axis=2
    ).astype(jnp.bfloat16)
    outgoing = jnp.dot(placed, normed_moe, preferred_element_type=jnp.float32).astype(jnp.bfloat16)
    outgoing = outgoing.reshape(capacity, expert_count, width)
    copies = jnp.broadcast_to(
        outgoing.reshape(capacity, exp_count, 1, local_exp, width),
        (capacity, exp_count, hid_count, local_exp, width),
    )
    copies = copies.reshape(capacity, exp_count * hid_count * local_exp, width)
    arrived = lax.all_to_all(copies, ("exp", "hid"), split_axis=1, concat_axis=0, tiled=True)
    partials = expert_rows(
        arrived, expert_gate_weight, expert_up_weight, expert_down_weight
    ).astype(jnp.bfloat16)
    returned = lax.all_to_all(partials, ("exp", "hid"), split_axis=0, concat_axis=1, tiled=True)
    returned = returned.reshape(capacity, exp_count, hid_count, local_exp, width)
    results = jnp.sum(returned.astype(jnp.float32), axis=2).astype(jnp.bfloat16)
    results = results.reshape(capacity * expert_count, width)
    picked = jnp.take(results, slots, axis=0).reshape(tok_rows, top_count, width)
    expert_out = jnp.sum(
        router_expert_weight[:, :, None] * picked.astype(jnp.float32), axis=1
    ).astype(jnp.bfloat16)
    return (attn_out, expert_out)


def solution(mesh):
    in_specs = (
        P(("req", "exp"), None),
        P(),
        P(None, "hid"),
        P(None, "hid"),
        P(None, "hid"),
        P("hid", None),
        P(("req", "exp"), None, None),
        P(("req", "exp"), None, None),
        P(("req", "exp"), None, None),
        P(("req", "exp"), None, None),
        P("req", None),
        P(),
        P(),
        P(),
        P(("req", "exp", "hid"), None),
        P(("req", "exp", "hid"), None),
        P("exp", None, "hid"),
        P("exp", None, "hid"),
        P("exp", "hid", None),
    )
    out_specs = (P(("req", "exp", "hid"), None), P(("req", "exp", "hid"), None))
    return jax.shard_map(
        per_device, mesh=mesh, in_specs=in_specs, out_specs=out_specs, check_vma=False
    )
```

profile of v0, /device:TPU:1, one launch (start us, length us, event | category | flops | bytes accessed | tf_op | source)
XLA Modules:
  0.0 728.0 jit_solution(7659078790844080535)
XLA Ops:
  15.1 1.7 fusion.82
  17.4 17.2 %all_gather.18 = bf16[2048,128]{0,1:T(8,128)(2,1)} all-gather(bf16[256,128]{0,1:T(8,128)(2,1)S(1)} %bitcast.138), channel_id=1, replica_groups=mesh['req'=8,'exp'=8,'hid'=4] {'exp'}, dimensions={0}, use_global_device_ids=true | all-gather | bytes 589824 | tf_op jit(solution)/shard_map/all_gather | solution.py:157
  35.2 56.6 %all-gather.11.cloned.1.call-done = bf16[64,16,512]{2,1,0:T(8,128)(2,1)} async-done(((bf16[1,16,512]{2,1,0:T(8,128)(2,1)}), bf16[64,16,512]{2,1,0:T(8,128)(2,1)}) %all-gather.11.cloned.1.call-update) | async-done | bytes 1048592 | tf_op jit(solution)/shard_map/all_gather | solution.py:109
  91.8 2.4 fusion.34
  94.2 76.1 %all-gather.5.cloned.1.call-done = bf16[64,1536,16]{1,2,0:T(8,128)(2,1)} async-done(((bf16[1,1536,16]{1,2,0:T(8,128)(2,1)}), bf16[64,1536,16]{1,2,0:T(8,128)(2,1)}) %all-gather.5.cloned.1.call-update) | async-done | bytes 3145744 | tf_op jit(solution)/shard_map/all_gather | solution.py:106
  170.3 5.3 fusion.12
  175.6 72.9 %all-gather.7.cloned.1.call-done = bf16[64,16,1536]{2,1,0:T(8,128)(2,1)} async-done(((bf16[1,16,1536]{2,1,0:T(8,128)(2,1)}), bf16[64,16,1536]{2,1,0:T(8,128)(2,1)}) %all-gather.7.cloned.1.call-update) | async-done | bytes 3145744 | tf_op jit(solution)/shard_map/all_gather | solution.py:107
  248.5 5.4 fusion.8
  256.1 1.9 copy.89
  259.1 7.7 %fusion = (f32[2,3,256]{2,1,0:T(4,128)S(1)}, f32[2,2048,256,3]{2,1,3,0:T(8,128)}) fusion(pred[256,2048]{0,1:T(8,128)(4,1)S(1)} %fusion.18, bf16[2048,2,64,1]{0,2,3,1:T(8,128)(2,1)} %bitcast.136, bf16[256,2,3,32]{0,3,2,1:T(8,128)(2,1)S(1)} %bitcast.144, bf16[256,2,3,32]{0,3,2,1:T(8,128)(2,1)S(1)} %bitcast.143), kind=kOutput, calls=%fused_computation.3 | convolution fusion | flops 412482048 | bytes 13834240 | tf_op jit(solution)/shard_map/qkgh,nkh->kgqn/dot_general | solution.py:166
  267.3 59.3 %all-gather.9.cloned.1.call-done = bf16[64,1536,16]{1,2,0:T(8,128)(2,1)} async-done(((bf16[1,1536,16]{1,2,0:T(8,128)(2,1)}), bf16[64,1536,16]{1,2,0:T(8,128)(2,1)}) %all-gather.9.cloned.1.call-update) | async-done | bytes 3145744 | tf_op jit(solution)/shard_map/all_gather | solution.py:108
  326.6 5.8 fusion.15
  333.6 13.2 %all_gather.23 = bf16[2048,128]{1,0:T(8,128)(2,1)S(1)} all-gather(bf16[256,128]{1,0:T(8,128)(2,1)S(1)} %fusion.33), channel_id=1, replica_groups=mesh['req'=8,'exp'=8,'hid'=4] {'exp'}, dimensions={0}, use_global_device_ids=true | all-gather | bytes 589824 | tf_op jit(solution)/shard_map/all_gather | solution.py:158
  347.0 7.5 %fusion.1 = f32[2,3,256]{2,1,0:T(4,128)S(1)} fusion(f32[2,2048,256,3]{2,1,3,0:T(8,128)} %get-tuple-element.11, f32[2,3,256]{2,1,0:T(4,128)} %broadcast_maximum_fusion, pred[256,2048]{0,1:T(8,128)(4,1)S(1)} %fusion.18), kind=kLoop, calls=%fused_computation.4 | loop fusion | flops 15727104 | bytes 13119488 | tf_op jit(solution)/shard_map/reduce_sum | solution.py:172
  355.3 3.6 fusion.39
  358.9 1.5 convolution_convert_fusion.1
  363.0 17.3 %reduce-scatter.2.cloned.1.call-done = bf16[64,1536]{1,0:T(8,128)(2,1)} async-done(((bf16[256,1536]{1,0:T(8,128)(2,1)}), bf16[64,1536]{1,0:T(8,128)(2,1)}) %reduce-scatter.2.cloned.1.call-update) | async-done | bytes 196624 | tf_op jit(solution)/shard_map/reduce_scatter | solution.py:183
  381.5 3.0 convolution_convert_fusion
  384.4 4.3 broadcast_in_dim.129
  388.7 3.2 copy.103
  392.8 98.3 %all_to_all.33 = bf16[16,160,1536]{2,0,1:T(8,128)(2,1)S(1)} all-to-all(bf16[16,160,1536]{2,0,1:T(8,128)(2,1)S(1)} %bitcast.131), channel_id=1, replica_groups=mesh['req'=8,'exp'=8,'hid'=4] {'exp','hid'}, dimensions={1} | all-to-all | bytes 15728640 | tf_op jit(solution)/shard_map/all_to_all | solution.py:216
  491.1 3.9 copy.104
  495.0 6.0 convolution_bitcast_fusion.1
  501.0 12.2 %convert_bitcast_fusion = bf16[512,5,1536]{2,0,1:T(8,128)(2,1)} fusion(bf16[5,128,1536]{2,1,0:T(8,128)(2,1)S(1)} %copy-done, bf16[512,5,1536]{2,0,1:T(8,128)(2,1)} %bitcast.134, bf16[5,1536,128]{2,1,0:T(8,128)(2,1)} %param.36, f32[512,5,128]{2,0,1:T(8,128)S(1)} %convolution_bitcast_fusion.1), kind=kOutput, calls=%fused_computation.6 | convolution fusion | flops 2019164160 | bytes 20971520 | tf_op jit(solution)/shard_map/ref,efd->red/dot_general | solution.py:59
  513.2 12.0 %copy.105 = bf16[512,5,1536]{2,1,0:T(8,128)(2,1)} copy(bf16[512,5,1536]{2,0,1:T(8,128)(2,1)} %convert_bitcast_fusion) | data formatting | bytes 15728640 | tf_op jit(solution)/shard_map/convert_element_type | solution.py:219
  525.1 5.6 all-to-all-start.1
  531.6 162.9 %all-to-all-done.1 = bf16[512,5,1536]{2,1,0:T(8,128)(2,1)} async-done(((bf16[512,5,1536]{2,1,0:T(8,128)(2,1)}), bf16[512,5,1536]{2,1,0:T(8,128)(2,1)}, u32[]{:S(2)}, u32[]{:S(2)}) %all-to-all-start.1) | async-done | bytes 7864352 | tf_op jit(solution)/shard_map/all_to_all | solution.py:220
  694.5 10.2 %reduce.1 = bf16[16,8,5,1536]{3,2,0,1:T(8,128)(2,1)} reduce(bf16[16,8,4,5,1536]{4,3,0,2,1:T(8,128)(2,1)} %bitcast.39, bf16[]{:T(256)} %constant.89.clone.1), dimensions={2}, to_apply=%region_14.15 | reduce | flops 2949120 | bytes 9830402 | tf_op jit(solution)/shard_map/reduce_sum | solution.py:222
  704.7 3.9 copy.107
  708.6 4.3 reshape.289
  712.9 5.5 gather_fusion
  718.4 2.8 multiply_reduce_fusion
  (105 shorter events, 20.4 us)
Async XLA Ops:
  7.2 493.8 %copy-start = (bf16[5,128,1536]{2,1,0:T(8,128)(2,1)S(1)}, bf16[5,128,1536]{2,1,0:T(8,128)(2,1)}, u32[]{:S(2)}) copy-start(bf16[5,128,1536]{2,1,0:T(8,128)(2,1)} %param.37) | copy-start | bytes 5898244
  7.2 84.6 %all-gather.11.cloned.1.call-start = ((), (), s32[]{:S(2)}) async-start(), calls=%async_computation.6 | async-start | bytes 1064960 | tf_op jit(solution)/shard_map/all_gather | solution.py:109
  7.9 162.4 %all-gather.5.cloned.1.call-start = ((), (), s32[]{:S(2)}) async-start(), calls=%async_computation.3 | async-start | bytes 3194880 | tf_op jit(solution)/shard_map/all_gather | solution.py:106
  8.7 239.9 %all-gather.7.cloned.1.call-start = ((), (), s32[]{:S(2)}) async-start(), calls=%async_computation.4 | async-start | bytes 3194880 | tf_op jit(solution)/shard_map/all_gather | solution.py:107
  9.4 317.2 %all-gather.9.cloned.1.call-start = ((), (), s32[]{:S(2)}) async-start(), calls=%async_computation.5 | async-start | bytes 3194880 | tf_op jit(solution)/shard_map/all_gather | solution.py:108
  10.0 370.3 %reduce-scatter.2.cloned.1.call-start = ((), (), s32[]{:S(2)}) async-start(), calls=%async_computation.7 | async-start | bytes 983040 | tf_op jit(solution)/shard_map/reduce_scatter | solution.py:183
  12.7 157.6 %copy-start.9 = (s32[4]{0:T(128)}, s32[4]{0:T(128)S(1)}, u32[]{:S(2)}) copy-start(s32[4]{0:T(128)S(1)} %select_reduce_fusion.1) | copy-start | bytes 52
  14.9 20.3 %copy-start.14 = (f32[256]{0:T(256)}, f32[256]{0:T(256)S(1)}, u32[]{:S(2)}) copy-start(f32[256]{0:T(256)S(1)} %add_rsqrt_fusion) | copy-start | bytes 3076
  175.6 78.3 %copy-start.3 = (bf16[256,1536]{1,0:T(8,128)(2,1)S(1)}, bf16[256,1536]{1,0:T(8,128)(2,1)}, u32[]{:S(2)}) copy-start(bf16[256,1536]{1,0:T(8,128)(2,1)} %param.19) | copy-start | bytes 2359300
  248.5 5.4 copy-start.15
  248.5 5.5 copy-start.19
  248.5 5.9 copy-start.11
  248.5 6.1 copy-start.17
  259.0 67.5 %copy-start.10 = (s32[4]{0:T(128)S(1)}, s32[4]{0:T(128)}, u32[]{:S(2)}) copy-start(s32[4]{0:T(128)} %copy-done.9) | copy-start | bytes 52
  266.7 65.7 %copy-start.16 = (f32[256]{0:T(256)S(1)}, f32[256]{0:T(256)}, u32[]{:S(2)}) copy-start(f32[256]{0:T(256)} %copy-done.14) | copy-start | bytes 3076
  266.7 65.7 %copy-start.20 = (f32[1536]{0:T(1024)S(1)}, f32[1536]{0:T(1024)}, u32[]{:S(2)}) copy-start(f32[1536]{0:T(1024)} %param.20) | copy-start | bytes 18436
  267.3 65.6 %copy-start.12 = (pred[256,4]{0,1:T(4,128)(4,1)S(1)}, pred[256,4]{0,1:T(4,128)(4,1)}, u32[]{:S(2)}) copy-start(pred[256,4]{0,1:T(4,128)(4,1)} %iota_compare_fusion.5) | copy-start | bytes 3076
  326.6 6.5 copy-start.18
  347.0 8.2 %copy-start.2 = (f32[2,2048,256,3]{2,1,3,0:T(8,128)S(1)}, f32[2,2048,256,3]{2,1,3,0:T(8,128)}, u32[]{:S(2)}) copy-start(f32[2,2048,256,3]{2,1,3,0:T(8,128)} %get-tuple-element.11) | copy-start | bytes 37748740
  347.0 8.2 %copy-start.6 = (f32[2,3,256]{2,1,0:T(4,128)S(1)}, f32[2,3,256]{2,1,0:T(4,128)}, u32[]{:S(2)}) copy-start(f32[2,3,256]{2,1,0:T(4,128)} %broadcast_maximum_fusion) | copy-start | bytes 18436
  355.2 3.6 copy-start.5
  358.9 1.5 copy-start.7
  358.9 21.5 %copy-start.4 = (bf16[256,1536]{1,0:T(8,128)(2,1)S(1)}, bf16[256,1536]{1,0:T(8,128)(2,1)}, u32[]{:S(2)}) copy-start(bf16[256,1536]{1,0:T(8,128)(2,1)} %param.19) | copy-start | bytes 2359300
  358.9 22.6 %copy-start.8 = (f32[1536]{0:T(1024)S(1)}, f32[1536]{0:T(1024)}, u32[]{:S(2)}) copy-start(f32[1536]{0:T(1024)} %param.32) | copy-start | bytes 18436
  525.1 5.8 copy-start.13
  525.1 169.4 %all-to-all-start.1 = ((bf16[512,5,1536]{2,1,0:T(8,128)(2,1)}), bf16[512,5,1536]{2,1,0:T(8,128)(2,1)}, u32[]{:S(2)}, u32[]{:S(2)}) async-start(bf16[512,5,1536]{2,1,0:T(8,128)(2,1)} %copy.105), calls=%async_computation.2 | async-start | bytes 25165824 | tf_op jit(solution)/shard_map/all_to_all | solution.py:220
  712.9 8.3 %copy-start.1 = (bf16[5,128,1536]{2,1,0:T(8,128)(2,1)S(1)}, bf16[5,128,1536]{2,1,0:T(8,128)(2,1)}, u32[]{:S(2)}) copy-start(bf16[5,128,1536]{2,1,0:T(8,128)(2,1)} %param.37) | copy-start | bytes 5898244
Sparse Core Ops, SparseCore 0:
  10.8 80.9 all-gather.10
  94.6 75.7 all-gather.4
  173.1 75.4 all-gather.6
  251.1 75.4 all-gather.8
  360.5 19.7 reduce-scatter.1
where the time goes:
time: 739 us; the launch traced here: 728 us
  waiting for transfers between devices  448 us (61%)
  blocking collectives  129 us (17%)
  matrix products  57.6 us (8%)
  local copies, waits for them, and re-layouts  43.5 us (6%)
  other arithmetic  30.3 us (4%)
  between operations  14.4 us (2%)
    all_to_all x1, waiting for transfers between devices, per_device(): lax.all_to_all(partials, ('exp', 'hid'), split_axis=0, concat_axis=1, til...  163 us
    all_to_all x1, blocking collectives, per_device(): lax.all_to_all(copies, ('exp', 'hid'), split_axis=1, concat_axis=0, tiled...  98.3 us
    all_gather x1, waiting for transfers between devices, per_device(): lax.all_gather(query_down_factor, ('req', 'exp'), axis=0, tiled=True)  76.1 us
    all_gather x1, waiting for transfers between devices, per_device(): lax.all_gather(query_up_factor, ('req', 'exp'), axis=0, tiled=True)  72.9 us
    all_gather x1, waiting for transfers between devices, per_device(): lax.all_gather(value_down_factor, ('req', 'exp'), axis=0, tiled=True)  59.3 us
    all_gather x1, waiting for transfers between devices, per_device(): lax.all_gather(value_up_factor, ('req', 'exp'), axis=0, tiled=True)  56.6 us
    dot_general x4, matrix products, per_device(): jnp.einsum('jn,nab->jab', selector, piece_in, preferred_element_type=jnp....  18.9 us
    reduce_scatter x1, waiting for transfers between devices, per_device(): lax.psum_scatter(jnp.dot(attended, attention_output_weight, preferred_ele...  17.3 us
  transfers between devices with their start and end apart: 6, of which 6 were waited for; matrix products, arithmetic and copies ran while one was open for 5% of the time, Pallas kernels for 0%

commit v1 on v0

--- a/solution.py
+++ b/solution.py
@@ -217,7 +217,15 @@
     partials = expert_rows(
         arrived, expert_gate_weight, expert_up_weight, expert_down_weight
     ).astype(jnp.bfloat16)
-    returned = lax.all_to_all(partials, ("exp", "hid"), split_axis=0, concat_axis=1, tiled=True)
+    returned = jnp.concatenate(
+        lax.all_to_all(
+            jnp.stack(jnp.split(partials, lax.axis_size(("exp", "hid")), axis=0)),
+            ("exp", "hid"),
+            0,
+            0,
+        ),
+        axis=1,
+    )
     returned = returned.reshape(capacity, exp_count, hid_count, local_exp, width)
     results = jnp.sum(returned.astype(jnp.float32), axis=2).astype(jnp.bfloat16)
     results = results.reshape(capacity * expert_count, width)

time: 739 us -> 706 us (0.955)
  waiting for transfers between devices: 448 us -> 374 us
  local copies, waits for them, and re-layouts: 43.5 us -> 84.2 us
    all_to_all x1, waiting for transfers between devices: 163 us -> 91 us  [per_device(): lax.all_to_all(jnp.stack(jnp.split(partials, lax.axis_size(('exp', 'hid')...]
    unnamed x44 -> x63, local copies, waits for them, and re-layouts: 1.6 us -> 53.1 us
    convert_element_type x1 -> x0, local copies, waits for them, and re-layouts: 12 us -> none  [per_device(): partials = expert_rows(arrived, expert_gate_weight, expert_up_weight, exp...]
  transfers between devices with their start and end apart: 6 -> 6, of which waited for: 6 -> 6; matrix products, arithmetic and copies ran while one was open for 5% -> 6% of each run, Pallas kernels for 0% -> 0%
where the time goes in v1:
time: 706 us; the launch traced here: 692 us
  waiting for transfers between devices  374 us (53%)
  blocking collectives  128 us (18%)
  local copies, waits for them, and re-layouts  84.2 us (12%)
  matrix products  61.2 us (9%)
  other arithmetic  24.4 us (3%)
  between operations  14.4 us (2%)
    all_to_all x1, blocking collectives, per_device(): lax.all_to_all(copies, ('exp', 'hid'), split_axis=1, concat_axis=0, tiled...  98 us
    all_to_all x1, waiting for transfers between devices, per_device(): lax.all_to_all(jnp.stack(jnp.split(partials, lax.axis_size(('exp', 'hid')...  91 us
    all_gather x1, waiting for transfers between devices, per_device(): lax.all_gather(query_down_factor, ('req', 'exp'), axis=0, tiled=True)  76.1 us
    all_gather x1, waiting for transfers between devices, per_device(): lax.all_gather(query_up_factor, ('req', 'exp'), axis=0, tiled=True)  72.9 us
    all_gather x1, waiting for transfers between devices, per_device(): lax.all_gather(value_down_factor, ('req', 'exp'), axis=0, tiled=True)  57.3 us
    all_gather x1, waiting for transfers between devices, per_device(): lax.all_gather(value_up_factor, ('req', 'exp'), axis=0, tiled=True)  56.6 us
    unnamed x63, local copies, waits for them, and re-layouts  53.1 us
    dot_general x4, matrix products, per_device(): jnp.einsum('jn,nab->jab', selector, piece_in, preferred_element_type=jnp....  18.8 us
  transfers between devices with their start and end apart: 6, of which 6 were waited for; matrix products, arithmetic and copies ran while one was open for 6% of the time, Pallas kernels for 0%

profile of v1, /device:TPU:1, one launch (start us, length us, event | category | flops | bytes accessed | tf_op | source)
XLA Modules:
  0.0 692.4 jit_solution(7970348818856229289)
XLA Ops:
  15.1 1.7 fusion.114
  17.5 17.2 %all_gather.18 = bf16[2048,128]{0,1:T(8,128)(2,1)} all-gather(bf16[256,128]{0,1:T(8,128)(2,1)S(1)} %bitcast.262), channel_id=1, replica_groups=mesh['req'=8,'exp'=8,'hid'=4] {'exp'}, dimensions={0}, use_global_device_ids=true | all-gather | bytes 589824 | tf_op jit(solution)/shard_map/all_gather | solution.py:157
  35.2 56.6 %all-gather.11.cloned.1.call-done = bf16[64,16,512]{2,1,0:T(8,128)(2,1)} async-done(((bf16[1,16,512]{2,1,0:T(8,128)(2,1)}), bf16[64,16,512]{2,1,0:T(8,128)(2,1)}) %all-gather.11.cloned.1.call-update) | async-done | bytes 1048592 | tf_op jit(solution)/shard_map/all_gather | solution.py:109
  91.8 2.4 fusion.34
  94.2 76.1 %all-gather.5.cloned.1.call-done = bf16[64,1536,16]{1,2,0:T(8,128)(2,1)} async-done(((bf16[1,1536,16]{1,2,0:T(8,128)(2,1)}), bf16[64,1536,16]{1,2,0:T(8,128)(2,1)}) %all-gather.5.cloned.1.call-update) | async-done | bytes 3145744 | tf_op jit(solution)/shard_map/all_gather | solution.py:106
  170.3 5.3 fusion.12
  175.7 72.9 %all-gather.7.cloned.1.call-done = bf16[64,16,1536]{2,1,0:T(8,128)(2,1)} async-done(((bf16[1,16,1536]{2,1,0:T(8,128)(2,1)}), bf16[64,16,1536]{2,1,0:T(8,128)(2,1)}) %all-gather.7.cloned.1.call-update) | async-done | bytes 3145744 | tf_op jit(solution)/shard_map/all_gather | solution.py:107
  248.5 5.3 fusion.8
  255.9 2.7 convolution_add_fusion
  258.6 1.9 copy.85
  261.6 7.7 %fusion = (f32[2,3,256]{2,1,0:T(4,128)S(1)}, f32[2,2048,256,3]{2,1,3,0:T(8,128)}) fusion(pred[256,2048]{0,1:T(8,128)(4,1)S(1)} %fusion.18, bf16[2048,2,64,1]{0,2,3,1:T(8,128)(2,1)} %bitcast.260, bf16[256,2,3,32]{0,3,2,1:T(8,128)(2,1)S(1)} %bitcast.268, bf16[256,2,3,32]{0,3,2,1:T(8,128)(2,1)S(1)} %bitcast.267), kind=kOutput, calls=%fused_computation.3 | convolution fusion | flops 412482048 | bytes 13834240 | tf_op jit(solution)/shard_map/qkgh,nkh->kgqn/dot_general | solution.py:166
  269.3 57.3 %all-gather.9.cloned.1.call-done = bf16[64,1536,16]{1,2,0:T(8,128)(2,1)} async-done(((bf16[1,1536,16]{1,2,0:T(8,128)(2,1)}), bf16[64,1536,16]{1,2,0:T(8,128)(2,1)}) %all-gather.9.cloned.1.call-update) | async-done | bytes 3145744 | tf_op jit(solution)/shard_map/all_gather | solution.py:108
  326.6 5.8 fusion.15
  334.5 13.2 %all_gather.23 = bf16[2048,128]{1,0:T(8,128)(2,1)S(1)} all-gather(bf16[256,128]{1,0:T(8,128)(2,1)S(1)} %fusion.33), channel_id=1, replica_groups=mesh['req'=8,'exp'=8,'hid'=4] {'exp'}, dimensions={0}, use_global_device_ids=true | all-gather | bytes 589824 | tf_op jit(solution)/shard_map/all_gather | solution.py:158
  348.8 7.4 %fusion.1 = f32[2,3,256]{2,1,0:T(4,128)S(1)} fusion(f32[2,2048,256,3]{2,1,3,0:T(8,128)} %get-tuple-element.11, f32[2,3,256]{2,1,0:T(4,128)S(1)} %broadcast_maximum_fusion, pred[256,2048]{0,1:T(8,128)(4,1)S(1)} %fusion.18), kind=kLoop, calls=%fused_computation.4 | loop fusion | flops 15727104 | bytes 13119488 | tf_op jit(solution)/shard_map/reduce_sum | solution.py:172
  357.1 3.6 fusion.39
  364.8 17.6 %reduce-scatter.2.cloned.1.call-done = bf16[64,1536]{1,0:T(8,128)(2,1)} async-done(((bf16[256,1536]{1,0:T(8,128)(2,1)}), bf16[64,1536]{1,0:T(8,128)(2,1)}) %reduce-scatter.2.cloned.1.call-update) | async-done | bytes 196624 | tf_op jit(solution)/shard_map/reduce_scatter | solution.py:183
  383.6 3.0 convolution_convert_fusion
  386.5 4.3 broadcast_in_dim.129
  390.8 3.2 copy.99
  394.9 98.0 %all_to_all.23 = bf16[16,160,1536]{2,0,1:T(8,128)(2,1)S(1)} all-to-all(bf16[16,160,1536]{2,0,1:T(8,128)(2,1)S(1)} %bitcast.255), channel_id=1, replica_groups=mesh['req'=8,'exp'=8,'hid'=4] {'exp','hid'}, dimensions={1} | all-to-all | bytes 15728640 | tf_op jit(solution)/shard_map/all_to_all | solution.py:216
  492.9 3.9 copy.100
  496.8 6.0 convolution_bitcast_fusion.1
  502.8 12.2 %convert_bitcast_fusion = bf16[512,5,1536]{2,0,1:T(8,128)(2,1)} fusion(bf16[5,128,1536]{2,1,0:T(8,128)(2,1)S(1)} %copy-done, bf16[512,5,1536]{2,0,1:T(8,128)(2,1)} %bitcast.258, bf16[5,1536,128]{2,1,0:T(8,128)(2,1)} %param.36, f32[512,5,128]{2,0,1:T(8,128)S(1)} %convolution_bitcast_fusion.1), kind=kOutput, calls=%fused_computation.7 | convolution fusion | flops 2019164160 | bytes 20971520 | tf_op jit(solution)/shard_map/ref,efd->red/dot_general | solution.py:59
  523.3 1.7 fusion.69
  568.1 5.5 all-to-all-start.1
  574.4 91.0 %all-to-all-done.1 = bf16[32,16,5,1536]{3,1,2,0:T(8,128)(2,1)} async-done(((bf16[32,16,5,1536]{3,1,2,0:T(8,128)(2,1)}), bf16[32,16,5,1536]{3,1,2,0:T(8,128)(2,1)}, u32[]{:S(2)}, u32[]{:S(2)}) %all-to-all-start.1) | async-done | bytes 7864352 | tf_op jit(solution)/shard_map/all_to_all | solution.py:221
  665.5 4.9 bitcast_reduce_fusion
  670.3 2.8 copy.101
  673.1 4.3 reshape.288
  677.4 5.4 gather_fusion
  682.8 2.8 multiply_reduce_fusion
  (124 shorter events, 74.6 us)
Async XLA Ops:
  7.2 495.6 %copy-start = (bf16[5,128,1536]{2,1,0:T(8,128)(2,1)S(1)}, bf16[5,128,1536]{2,1,0:T(8,128)(2,1)}, u32[]{:S(2)}) copy-start(bf16[5,128,1536]{2,1,0:T(8,128)(2,1)} %param.37) | copy-start | bytes 5898244
  7.2 246.7 %copy-start.2 = (bf16[256,1536]{1,0:T(8,128)(2,1)S(1)}, bf16[256,1536]{1,0:T(8,128)(2,1)}, u32[]{:S(2)}) copy-start(bf16[256,1536]{1,0:T(8,128)(2,1)} %param.19) | copy-start | bytes 2359300
  7.2 84.6 %all-gather.11.cloned.1.call-start = ((), (), s32[]{:S(2)}) async-start(), calls=%async_computation.6 | async-start | bytes 1064960 | tf_op jit(solution)/shard_map/all_gather | solution.py:109
  7.9 162.4 %all-gather.5.cloned.1.call-start = ((), (), s32[]{:S(2)}) async-start(), calls=%async_computation.3 | async-start | bytes 3194880 | tf_op jit(solution)/shard_map/all_gather | solution.py:106
  8.7 239.9 %all-gather.7.cloned.1.call-start = ((), (), s32[]{:S(2)}) async-start(), calls=%async_computation.4 | async-start | bytes 3194880 | tf_op jit(solution)/shard_map/all_gather | solution.py:107
  9.4 317.2 %all-gather.9.cloned.1.call-start = ((), (), s32[]{:S(2)}) async-start(), calls=%async_computation.5 | async-start | bytes 3194880 | tf_op jit(solution)/shard_map/all_gather | solution.py:108
  10.0 372.4 %reduce-scatter.2.cloned.1.call-start = ((), (), s32[]{:S(2)}) async-start(), calls=%async_computation.7 | async-start | bytes 983040 | tf_op jit(solution)/shard_map/reduce_scatter | solution.py:183
  12.7 157.6 %copy-start.8 = (s32[4]{0:T(128)}, s32[4]{0:T(128)S(1)}, u32[]{:S(2)}) copy-start(s32[4]{0:T(128)S(1)} %select_reduce_fusion.1) | copy-start | bytes 52
  14.9 19.8 %copy-start.12 = (f32[256]{0:T(256)}, f32[256]{0:T(256)S(1)}, u32[]{:S(2)}) copy-start(f32[256]{0:T(256)S(1)} %add_rsqrt_fusion) | copy-start | bytes 3076
  258.6 68.0 %copy-start.9 = (s32[4]{0:T(128)S(1)}, s32[4]{0:T(128)}, u32[]{:S(2)}) copy-start(s32[4]{0:T(128)} %copy-done.8) | copy-start | bytes 52
  261.6 70.8 %copy-start.13 = (f32[256]{0:T(256)S(1)}, f32[256]{0:T(256)}, u32[]{:S(2)}) copy-start(f32[256]{0:T(256)} %copy-done.12) | copy-start | bytes 3076
  261.6 70.8 %copy-start.14 = (f32[1536]{0:T(1024)S(1)}, f32[1536]{0:T(1024)}, u32[]{:S(2)}) copy-start(f32[1536]{0:T(1024)} %param.20) | copy-start | bytes 18436
  261.6 71.2 %copy-start.10 = (pred[256,4]{0,1:T(4,128)(4,1)S(1)}, pred[256,4]{0,1:T(4,128)(4,1)}, u32[]{:S(2)}) copy-start(pred[256,4]{0,1:T(4,128)(4,1)} %iota_compare_fusion.5) | copy-start | bytes 3076
  348.8 8.2 %copy-start.1 = (f32[2,2048,256,3]{2,1,3,0:T(8,128)S(1)}, f32[2,2048,256,3]{2,1,3,0:T(8,128)}, u32[]{:S(2)}) copy-start(f32[2,2048,256,3]{2,1,3,0:T(8,128)} %get-tuple-element.11) | copy-start | bytes 37748740
  348.8 8.3 %copy-start.5 = (bf16[2048,128]{0,1:T(8,128)(2,1)S(1)}, bf16[2048,128]{0,1:T(8,128)(2,1)}, u32[]{:S(2)}) copy-start(bf16[2048,128]{0,1:T(8,128)(2,1)} %copy.90) | copy-start | bytes 1572868
  357.0 3.6 copy-start.4
  357.0 5.1 copy-start.6
  357.0 25.4 %copy-start.3 = (bf16[256,1536]{1,0:T(8,128)(2,1)S(1)}, bf16[256,1536]{1,0:T(8,128)(2,1)}, u32[]{:S(2)}) copy-start(bf16[256,1536]{1,0:T(8,128)(2,1)} %param.19) | copy-start | bytes 2359300
  357.1 26.5 %copy-start.7 = (f32[1536]{0:T(1024)S(1)}, f32[1536]{0:T(1024)}, u32[]{:S(2)}) copy-start(f32[1536]{0:T(1024)} %param.32) | copy-start | bytes 18436
  568.1 5.7 copy-start.11
  568.1 97.4 %all-to-all-start.1 = ((bf16[32,16,5,1536]{3,1,2,0:T(8,128)(2,1)}), bf16[32,16,5,1536]{3,1,2,0:T(8,128)(2,1)}, u32[]{:S(2)}, u32[]{:S(2)}) async-start(bf16[32,16,5,1536]{3,1,2,0:T(8,128)(2,1)} %fusion.43), calls=%async_computation.2 | async-start | bytes 15728640 | tf_op jit(solution)/shard_map/all_to_all | solution.py:221
Sparse Core Ops, SparseCore 0:
  10.8 80.9 all-gather.10
  94.6 75.7 all-gather.4
  173.1 75.4 all-gather.6
  251.1 75.4 all-gather.8
  362.3 20.0 reduce-scatter.1
